TPU v7x, 128 devices: a whole 4x4x4 slice. The times are simulated.
128 devices in a mesh: space: 32 (over x, z, core), feat: 4 (over y).
Axes of the slice: x: 4, y: 4, z: 4, core: 2. Of those that a mesh axis runs over, the one named last changes fastest.
Arguments:
- inputs: bfloat16 [2, 96, 180, 1024], P(None, 'space', None, 'feat'), may hold values from -15 to 15
- cotangent: bfloat16 [2, 96, 180, 1024], P(None, 'space', None, 'feat'), may hold values from -6 to 6
- spec_w1: float32 [2, 8, 128, 128], P(None, 'feat'), may hold values from -0.375 to 0.375
- spec_b1: float32 [2, 1024], P(None, 'feat'), may hold values from -0.3 to 0.3
- spec_w2: float32 [2, 8, 128, 128], P(None, 'feat'), may hold values from -0.375 to 0.375
- spec_b2: float32 [2, 1024], P(None, 'feat'), may hold values from -0.3 to 0.3
- up_weight: bfloat16 [1024, 4096], P(None, 'feat'), may hold values from -0.1875 to 0.1875
- down_weight: bfloat16 [4096, 1024], P('feat'), may hold values from -0.09375 to 0.09375
Outputs:
- output: bfloat16 [2, 96, 180, 1024], P(None, 'space', None, 'feat')
- grad_input: bfloat16 [2, 96, 180, 1024], P(None, 'space', None, 'feat')
All inputs are finite; a program needn't handle non-finite values.
Results may differ from a plain program's by a relative error of at most 0.0102.
Values may be sent and summed in bfloat16 or wider, within the bound.
No kernel may reach another device: no remote copies, remote signals or barrier semaphores. Data moves between devices by JAX's collectives and lax.ppermute only.
A program may use at most 128 MiB of HBM per device.

v0:
```python
import math

import jax
import jax.numpy as jnp
from jax import lax
from jax.sharding import PartitionSpec as P

EPSILON = 1e-05
SHRINK_LEVEL = 0.1
HIGHEST = lax.Precision.HIGHEST


def swapped(block, axis, bit):
    count = lax.axis_size(axis)
    route = []
    for low in range(count):
        high = low | 1 << bit
        if high != low and high < count:
            route += [(low, high), (high, low)]
    return lax.ppermute(block, axis, route)


def longitude_tables(width_lon):
    mode_count = width_lon // 2 + 1
    cell_index = jnp.arange(width_lon, dtype=jnp.int32)[:, None]
    wave_number = jnp.arange(mode_count, dtype=jnp.int32)[None, :]
    phase_angle = (
        2.0 * math.pi / width_lon * (cell_index * wave_number % width_lon).astype(jnp.float32)
    )
    scaling = 1.0 / math.sqrt(width_lon)
    cos_fwd = jnp.cos(phase_angle) * scaling
    sin_fwd = -jnp.sin(phase_angle) * scaling
    doubled = jnp.where((wave_number == 0) | (wave_number * 2 == width_lon), 1.0, 2.0).astype(
        jnp.float32
    )
    return (cos_fwd, sin_fwd, cos_fwd * doubled, sin_fwd * doubled)


def padded_tables(width_lon):
    tables = longitude_tables(width_lon)
    return tables


def lat_apply(table, field):
    return jnp.einsum("gh,bhkc->bgkc", table, field, precision=HIGHEST)


def complex_latitude(table_cos, table_sin, real_part, imag_part, inverse):
    if inverse:
        return (
            lat_apply(table_cos, real_part) + lat_apply(table_sin, imag_part),
            lat_apply(table_cos, imag_part) - lat_apply(table_sin, real_part),
        )
    return (
        lat_apply(table_cos, real_part) - lat_apply(table_sin, imag_part),
        lat_apply(table_cos, imag_part) + lat_apply(table_sin, real_part),
    )


def lon_forward(field, table):
    return jnp.einsum("brwc,wk->brkc", field, table, precision=HIGHEST)


def lon_back(spec, table):
    return jnp.einsum("brkc,wk->brwc", spec, table, precision=HIGHEST)


def to_blocks(field, block_size):
    return field.reshape(field.shape[:-1] + (field.shape[-1] // block_size, block_size))


def block_mult(field, weights):
    return jnp.einsum("...nc,nce->...ne", field, weights, precision=HIGHEST)


def block_mult_back(field, weights):
    return jnp.einsum("...ne,nce->...nc", field, weights, precision=HIGHEST)


def block_product(real_part, imag_part, weights):
    return (
        block_mult(real_part, weights[0]) - block_mult(imag_part, weights[1]),
        block_mult(real_part, weights[1]) + block_mult(imag_part, weights[0]),
    )


def block_adjoint(real_part, imag_part, weights):
    return (
        block_mult_back(real_part, weights[0]) + block_mult_back(imag_part, weights[1]),
        block_mult_back(imag_part, weights[0]) - block_mult_back(real_part, weights[1]),
    )


def butterfly_level(real_part, imag_part, position, level_bit, inverse):
    half_span = 1 << level_bit
    is_upper = position >> level_bit & 1 == 1
    offset = (position & half_span - 1).astype(jnp.float32)
    phase_angle = math.pi / half_span * offset
    cosine = jnp.cos(phase_angle)
    sine_val = jnp.sin(phase_angle)
    turned_real = real_part * cosine - imag_part * sine_val
    turned_imag = imag_part * cosine + real_part * sine_val
    if inverse:
        outgoing = jnp.stack(
            [
                jnp.where(is_upper, turned_real, real_part),
                jnp.where(is_upper, turned_imag, imag_part),
            ]
        )
    else:
        outgoing = jnp.stack([real_part, imag_part])
    received = swapped(outgoing, "space", level_bit)
    got_real = received[0]
    got_imag = received[1]
    if inverse:
        upper_real = got_real - turned_real
        upper_imag = got_imag - turned_imag
    else:
        diff_real = got_real - real_part
        diff_imag = got_imag - imag_part
        upper_real = diff_real * cosine + diff_imag * sine_val
        upper_imag = diff_imag * cosine - diff_real * sine_val
    return (
        jnp.where(is_upper, upper_real, real_part + got_real),
        jnp.where(is_upper, upper_imag, imag_part + got_imag),
    )


def butterfly_transform(real_part, imag_part, inverse):
    nspace = lax.axis_size("space")
    levels = nspace.bit_length() - 1
    position = lax.axis_index("space")
    row_count = real_part.shape[1]
    length = row_count * nspace
    frequency = jnp.zeros((), jnp.int32)
    for level_bit in range(levels):
        frequency = frequency + ((position >> level_bit & 1) << levels - 1 - level_bit)
    out_index = jnp.arange(row_count, dtype=jnp.int32)[:, None]
    in_index = jnp.arange(row_count, dtype=jnp.int32)[None, :]
    wave_number = frequency + nspace * out_index
    phase_angle = 2.0 * math.pi / length * (wave_number * in_index % length).astype(jnp.float32)
    scaling = 1.0 / math.sqrt(length)
    table_cos = jnp.cos(phase_angle) * scaling
    table_sin = -jnp.sin(phase_angle) * scaling
    if inverse:
        real_part, imag_part = complex_latitude(
            table_cos.T, table_sin.T, real_part, imag_part, True
        )
        for level_bit in range(levels):
            real_part, imag_part = butterfly_level(real_part, imag_part, position, level_bit, True)
        return (real_part, imag_part)
    for level_bit in reversed(range(levels)):
        real_part, imag_part = butterfly_level(real_part, imag_part, position, level_bit, False)
    return complex_latitude(table_cos, table_sin, real_part, imag_part, False)


def enter_spectrum(real_part, imag_part):
    result = butterfly_transform(real_part, imag_part, False)
    return result


def leave_spectrum(real_part, imag_part):
    result = butterfly_transform(real_part, imag_part, True)
    return result


def token_sums(first_term, second_term):
    return lax.psum((first_term, second_term), "feat")


def channel_share(term):
    return lax.psum_scatter(
        term.astype(jnp.bfloat16), "feat", scatter_dimension=3, tiled=True
    ).astype(jnp.float32)


def gelu_value(field):
    return 0.5 * field * (1.0 + lax.erf(field * (1.0 / math.sqrt(2.0))))


def gelu_slope(field):
    return 0.5 * (1.0 + lax.erf(field * (1.0 / math.sqrt(2.0)))) + field * jnp.exp(
        -0.5 * field * field
    ) * (1.0 / math.sqrt(2.0 * math.pi))


def per_device(inputs, cotangent, spec_w1, spec_b1, spec_w2, spec_b2, up_weight, down_weight):
    full_width = up_weight.shape[0]
    block_size = spec_w1.shape[2]
    cos_fwd, sin_fwd, cos_inv, sin_inv = padded_tables(inputs.shape[2])
    values = inputs.astype(jnp.float32)
    first_sum, second_sum = token_sums(jnp.sum(values, axis=-1), jnp.sum(values * values, axis=-1))
    mean_one = first_sum[..., None] / full_width
    rstd_one = lax.rsqrt(second_sum[..., None] / full_width - mean_one * mean_one + EPSILON)
    normed = (values - mean_one) * rstd_one
    spec_real, spec_imag = enter_spectrum(
        lon_forward(normed, cos_fwd), lon_forward(normed, sin_fwd)
    )
    spec_shape = spec_real.shape
    bias_one = to_blocks(spec_b1, block_size)
    bias_two = to_blocks(spec_b2, block_size)
    first_real, first_imag = block_product(
        to_blocks(spec_real, block_size), to_blocks(spec_imag, block_size), spec_w1
    )
    first_real = jax.nn.relu(first_real + bias_one[0])
    first_imag = jax.nn.relu(first_imag + bias_one[1])
    second_real, second_imag = block_product(first_real, first_imag, spec_w2)
    second_real = second_real + bias_two[0]
    second_imag = second_imag + bias_two[1]
    shrunk_real = (second_real - jnp.clip(second_real, -SHRINK_LEVEL, SHRINK_LEVEL)).reshape(
        spec_shape
    )
    shrunk_imag = (second_imag - jnp.clip(second_imag, -SHRINK_LEVEL, SHRINK_LEVEL)).reshape(
        spec_shape
    )
    back_real, back_imag = leave_spectrum(shrunk_real, shrunk_imag)
    filtered = lon_back(back_real, cos_inv) + lon_back(back_imag, sin_inv)
    residual = (filtered + normed + values).astype(jnp.bfloat16)
    residual_vals = residual.astype(jnp.float32)
    whole_residual, whole_cotangent = (
        lax.all_gather(residual, "feat", axis=3, tiled=True),
        lax.all_gather(cotangent, "feat", axis=3, tiled=True),
    )
    whole_vals = whole_residual.astype(jnp.float32)
    mean_two = jnp.sum(whole_vals, axis=-1, keepdims=True) / full_width
    square_two = jnp.sum(whole_vals * whole_vals, axis=-1, keepdims=True) / full_width
    rstd_two = lax.rsqrt(square_two - mean_two * mean_two + EPSILON)
    vhat = (whole_vals - mean_two) * rstd_two
    hidden = jnp.einsum(
        "brwd,dh->brwh", vhat.astype(jnp.bfloat16), up_weight, preferred_element_type=jnp.float32
    )
    activated = gelu_value(hidden).astype(jnp.bfloat16)
    mixed_term = jnp.einsum(
        "brwh,hd->brwd", activated, down_weight, preferred_element_type=jnp.float32
    )
    output = (residual_vals + channel_share(mixed_term)).astype(jnp.bfloat16)
    grad_act = jnp.einsum(
        "brwd,hd->brwh", whole_cotangent, down_weight, preferred_element_type=jnp.float32
    )
    grad_hidden = (grad_act * gelu_slope(hidden)).astype(jnp.bfloat16)
    grad_term = jnp.einsum(
        "brwh,dh->brwd", grad_hidden, up_weight, preferred_element_type=jnp.float32
    )
    grad_vhat = channel_share(grad_term)
    own_hat = (residual_vals - mean_two) * rstd_two
    total_one, total_two = token_sums(
        jnp.sum(grad_vhat, axis=-1), jnp.sum(grad_vhat * own_hat, axis=-1)
    )
    grad_residual = cotangent.astype(jnp.float32) + rstd_two * (
        grad_vhat
        - total_one[..., None] / full_width
        - own_hat * (total_two[..., None] / full_width)
    )
    grad_real, grad_imag = enter_spectrum(
        lon_forward(grad_residual, cos_inv), lon_forward(grad_residual, sin_inv)
    )
    grad_real = jnp.where(
        jnp.abs(second_real) > SHRINK_LEVEL, to_blocks(grad_real, block_size), 0.0
    )
    grad_imag = jnp.where(
        jnp.abs(second_imag) > SHRINK_LEVEL, to_blocks(grad_imag, block_size), 0.0
    )
    first_grad_real, first_grad_imag = block_adjoint(grad_real, grad_imag, spec_w2)
    first_grad_real = jnp.where(first_real > 0.0, first_grad_real, 0.0)
    first_grad_imag = jnp.where(first_imag > 0.0, first_grad_imag, 0.0)
    spec_grad_real, spec_grad_imag = block_adjoint(first_grad_real, first_grad_imag, spec_w1)
    rows_real, rows_imag = leave_spectrum(
        spec_grad_real.reshape(spec_shape), spec_grad_imag.reshape(spec_shape)
    )
    grad_normed = grad_residual + lon_back(rows_real, cos_fwd) + lon_back(rows_imag, sin_fwd)
    norm_one, norm_two = token_sums(
        jnp.sum(grad_normed, axis=-1), jnp.sum(grad_normed * normed, axis=-1)
    )
    grad_input = grad_residual + rstd_one * (
        grad_normed - norm_one[..., None] / full_width - normed * (norm_two[..., None] / full_width)
    )
    return (output, grad_input.astype(jnp.bfloat16))


def solution(mesh):
    return jax.shard_map(
        per_device,
        mesh=mesh,
        in_specs=(
            P(None, "space", None, "feat"),
            P(None, "space", None, "feat"),
            P(None, "feat", None, None),
            P(None, "feat"),
            P(None, "feat", None, None),
            P(None, "feat"),
            P(None, "feat"),
            P("feat", None),
        ),
        out_specs=(P(None, "space", None, "feat"), P(None, "space", None, "feat")),
        check_vma=False,
    )
```

profile of v0, /device:TPU:0, one launch (start us, length us, event | category | flops | bytes accessed | tf_op | source)
XLA Modules:
  0.0 733.5 jit_solution(15299313492322375288)
XLA Ops:
  9.0 17.3 %all-reduce.2 = (f32[2,3,180]{2,1,0:T(4,128)S(1)}, f32[2,3,180]{2,1,0:T(4,128)S(1)}) all-reduce(f32[2,3,180]{2,1,0:T(4,128)S(1)} %get-tuple-element.15, f32[2,3,180]{2,1,0:T(4,128)S(1)} %get-tuple-element.14), channel_id=1, replica_groups=mesh['space'=32,'feat'=4] {'feat'}, use_global_device_ids=true, to_apply=%region_3.4 | all-reduce | flops 2160 | bytes 17280 | tf_op jit(solution)/shard_map/psum | solution.py:168
  32.8 3.0 collective-permute-start
  36.0 21.2 %collective-permute-done = f32[2,2,3,91,256]{4,1,3,2,0:T(2,128)S(1)} collective-permute-done((f32[2,2,3,91,256]{4,1,3,2,0:T(2,128)}, f32[2,2,3,91,256]{4,1,3,2,0:T(2,128)S(1)}, u32[]{:S(2)}, u32[]{:S(2)}) %collective-permute-start) | collective-permute-done | bytes 1118240 | tf_op jit(solution)/shard_map/ppermute | solution.py:20
  62.7 20.4 %collective-permute-done.1 = f32[2,2,3,91,256]{4,1,3,2,0:T(2,128)} collective-permute-done((f32[2,2,3,91,256]{4,1,3,2,0:T(2,128)}, f32[2,2,3,91,256]{4,1,3,2,0:T(2,128)}, u32[]{:S(2)}, u32[]{:S(2)}) %collective-permute-start.1) | collective-permute-done | bytes 1118240 | tf_op jit(solution)/shard_map/ppermute | solution.py:20
  88.0 3.9 collective-permute-start.2
  92.0 19.2 %collective-permute-done.2 = f32[2,2,3,91,256]{4,1,3,2,0:T(2,128)} collective-permute-done((f32[2,2,3,91,256]{4,1,3,2,0:T(2,128)}, f32[2,2,3,91,256]{4,1,3,2,0:T(2,128)}, u32[]{:S(2)}, u32[]{:S(2)}) %collective-permute-start.2) | collective-permute-done | bytes 1118240 | tf_op jit(solution)/shard_map/ppermute | solution.py:20
  117.6 19.0 %collective-permute-done.3 = f32[2,2,3,91,256]{4,1,3,2,0:T(2,128)} collective-permute-done((f32[2,2,3,91,256]{4,1,3,2,0:T(2,128)}, f32[2,2,3,91,256]{4,1,3,2,0:T(2,128)}, u32[]{:S(2)}, u32[]{:S(2)}) %collective-permute-start.3) | collective-permute-done | bytes 1118240 | tf_op jit(solution)/shard_map/ppermute | solution.py:20
  148.5 2.6 fusion.84
  152.8 2.6 fusion.45
  160.0 2.6 fusion.44
  173.2 2.5 reshape.130
  175.7 3.5 fusion.275
  184.2 2.5 reshape.131
  186.7 2.7 fusion.287
  193.0 2.6 collective-permute-done.5
  198.4 25.6 %collective-permute-done.6 = f32[2,2,3,91,256]{4,1,3,2,0:T(2,128)S(1)} collective-permute-done((f32[2,2,3,91,256]{4,1,3,2,0:T(2,128)S(1)}, f32[2,2,3,91,256]{4,1,3,2,0:T(2,128)S(1)}, u32[]{:S(2)}, u32[]{:S(2)}) %collective-permute-start.6) | collective-permute-done | bytes 1118240 | tf_op jit(solution)/shard_map/ppermute | solution.py:20
  225.9 3.0 collective-permute-start.7
  228.9 24.4 %collective-permute-done.7 = f32[2,2,3,91,256]{4,1,3,2,0:T(2,128)S(1)} collective-permute-done((f32[2,2,3,91,256]{4,1,3,2,0:T(2,128)S(1)}, f32[2,2,3,91,256]{4,1,3,2,0:T(2,128)S(1)}, u32[]{:S(2)}, u32[]{:S(2)}) %collective-permute-start.7) | collective-permute-done | bytes 1118240 | tf_op jit(solution)/shard_map/ppermute | solution.py:20
  256.7 23.4 %collective-permute-done.8 = f32[2,2,3,91,256]{4,1,3,2,0:T(2,128)S(1)} collective-permute-done((f32[2,2,3,91,256]{4,1,3,2,0:T(2,128)S(1)}, f32[2,2,3,91,256]{4,1,3,2,0:T(2,128)S(1)}, u32[]{:S(2)}, u32[]{:S(2)}) %collective-permute-start.8) | collective-permute-done | bytes 1118240 | tf_op jit(solution)/shard_map/ppermute | solution.py:20
  281.9 3.2 collective-permute-start.9
  285.0 22.4 %collective-permute-done.9 = f32[2,2,3,91,256]{4,1,3,2,0:T(2,128)S(1)} collective-permute-done((f32[2,2,3,91,256]{4,1,3,2,0:T(2,128)S(1)}, f32[2,2,3,91,256]{4,1,3,2,0:T(2,128)S(1)}, u32[]{:S(2)}, u32[]{:S(2)}) %collective-permute-start.9) | collective-permute-done | bytes 1118240 | tf_op jit(solution)/shard_map/ppermute | solution.py:20
  309.4 2.6 fusion.41
  314.3 33.0 %all-gather.3.cloned.1.call-done = bf16[2,3,180,1024]{3,2,1,0:T(8,128)(2,1)} async-done(((bf16[2,3,180,256]{3,2,1,0:T(8,128)(2,1)}), bf16[2,3,180,1024]{3,2,1,0:T(8,128)(2,1)}) %all-gather.3.cloned.1.call-update) | async-done | bytes 2211856 | tf_op jit(solution)/shard_map/all_gather | solution.py:221
  347.3 2.5 convert_reduce_fusion
  350.5 5.0 fusion.12
  355.5 30.4 %all-gather.5.cloned.1.call-done = bf16[2,3,180,1024]{3,2,1,0:T(8,128)(2,1)} async-done(((bf16[2,3,180,256]{3,2,1,0:T(8,128)(2,1)}), bf16[2,3,180,1024]{3,2,1,0:T(8,128)(2,1)}) %all-gather.5.cloned.1.call-update) | async-done | bytes 2211856 | tf_op jit(solution)/shard_map/all_gather | solution.py:222
  385.8 9.8 %fusion.28 = bf16[2,3,180,1024]{3,2,1,0:T(8,128)(2,1)} fusion(bf16[1024,1024]{1,0:T(8,128)(2,1)S(1)} %copy-done, f32[2,3,180,1024]{3,2,1,0:T(8,128)} %fusion.12, bf16[2,3,180,1024]{3,2,1,0:T(8,128)(2,1)} %all-gather.5.cloned.1.call-done, bf16[1024,1024]{1,0:T(8,128)(2,1)} %param.15), kind=kOutput, calls=%fused_computation.34 | convolution fusion | flops 4542013440 | bytes 13041664 | tf_op jit(solution)/shard_map/brwh,dh->brwd/dot_general | solution.py:241
  395.7 32.1 %reduce-scatter.5.cloned.1.call-done = bf16[2,3,180,256]{3,2,1,0:T(8,128)(2,1)} async-done(((bf16[2,3,180,1024]{3,2,1,0:T(8,128)(2,1)}), bf16[2,3,180,256]{3,2,1,0:T(8,128)(2,1)}) %reduce-scatter.5.cloned.1.call-update) | async-done | bytes 552976 | tf_op jit(solution)/shard_map/reduce_scatter | solution.py:172
  429.8 15.0 %all-reduce.1 = (f32[2,3,180]{2,1,0:T(4,128)S(1)}, f32[2,3,180]{2,1,0:T(4,128)S(1)}) all-reduce(f32[2,3,180]{2,1,0:T(4,128)S(1)} %get-tuple-element.13, f32[2,3,180]{2,1,0:T(4,128)S(1)} %get-tuple-element.12), channel_id=1, replica_groups=mesh['space'=32,'feat'=4] {'feat'}, use_global_device_ids=true, to_apply=%region_11.12 | all-reduce | flops 2160 | bytes 17280 | tf_op jit(solution)/shard_map/psum | solution.py:168
  449.1 3.3 collective-permute-start.10
  452.4 21.2 %collective-permute-done.10 = f32[2,2,3,91,256]{4,1,3,2,0:T(2,128)S(1)} collective-permute-done((f32[2,2,3,91,256]{4,1,3,2,0:T(2,128)S(1)}, f32[2,2,3,91,256]{4,1,3,2,0:T(2,128)S(1)}, u32[]{:S(2)}, u32[]{:S(2)}) %collective-permute-start.10) | collective-permute-done | bytes 1118240 | tf_op jit(solution)/shard_map/ppermute | solution.py:20
  476.7 20.8 %collective-permute-done.11 = f32[2,2,3,91,256]{4,1,3,2,0:T(2,128)S(1)} collective-permute-done((f32[2,2,3,91,256]{4,1,3,2,0:T(2,128)S(1)}, f32[2,2,3,91,256]{4,1,3,2,0:T(2,128)S(1)}, u32[]{:S(2)}, u32[]{:S(2)}) %collective-permute-start.11) | collective-permute-done | bytes 1118240 | tf_op jit(solution)/shard_map/ppermute | solution.py:20
  499.2 3.2 collective-permute-start.12
  502.4 20.7 %collective-permute-done.12 = f32[2,2,3,91,256]{4,1,3,2,0:T(2,128)S(1)} collective-permute-done((f32[2,2,3,91,256]{4,1,3,2,0:T(2,128)S(1)}, f32[2,2,3,91,256]{4,1,3,2,0:T(2,128)S(1)}, u32[]{:S(2)}, u32[]{:S(2)}) %collective-permute-start.12) | collective-permute-done | bytes 1118240 | tf_op jit(solution)/shard_map/ppermute | solution.py:20
  526.1 20.2 %collective-permute-done.13 = f32[2,2,3,91,256]{4,1,3,2,0:T(2,128)S(1)} collective-permute-done((f32[2,2,3,91,256]{4,1,3,2,0:T(2,128)S(1)}, f32[2,2,3,91,256]{4,1,3,2,0:T(2,128)S(1)}, u32[]{:S(2)}, u32[]{:S(2)}) %collective-permute-start.13) | collective-permute-done | bytes 1118240 | tf_op jit(solution)/shard_map/ppermute | solution.py:20
  548.5 2.7 collective-permute-done.14
  553.6 2.6 fusion.82
  556.2 2.6 fusion.42
  560.4 3.7 fusion.43
  584.5 2.6 collective-permute-done.15
  590.3 25.3 %collective-permute-done.16 = f32[2,2,3,91,256]{4,1,3,2,0:T(2,128)S(1)} collective-permute-done((f32[2,2,3,91,256]{4,1,3,2,0:T(2,128)S(1)}, f32[2,2,3,91,256]{4,1,3,2,0:T(2,128)S(1)}, u32[]{:S(2)}, u32[]{:S(2)}) %collective-permute-start.16) | collective-permute-done | bytes 1118240 | tf_op jit(solution)/shard_map/ppermute | solution.py:20
  619.4 25.5 %collective-permute-done.17 = f32[2,2,3,91,256]{4,1,3,2,0:T(2,128)S(1)} collective-permute-done((f32[2,2,3,91,256]{4,1,3,2,0:T(2,128)S(1)}, f32[2,2,3,91,256]{4,1,3,2,0:T(2,128)S(1)}, u32[]{:S(2)}, u32[]{:S(2)}) %collective-permute-start.17) | collective-permute-done | bytes 1118240 | tf_op jit(solution)/shard_map/ppermute | solution.py:20
  649.2 3.7 fusion.25
  652.9 19.9 %collective-permute-done.18 = f32[2,2,3,91,256]{4,1,3,2,0:T(2,128)S(1)} collective-permute-done((f32[2,2,3,91,256]{4,1,3,2,0:T(2,128)}, f32[2,2,3,91,256]{4,1,3,2,0:T(2,128)S(1)}, u32[]{:S(2)}, u32[]{:S(2)}) %collective-permute-start.18) | collective-permute-done | bytes 1118240 | tf_op jit(solution)/shard_map/ppermute | solution.py:20
  676.5 24.1 %collective-permute-done.19 = f32[2,2,3,91,256]{4,1,3,2,0:T(2,128)S(1)} collective-permute-done((f32[2,2,3,91,256]{4,1,3,2,0:T(2,128)S(1)}, f32[2,2,3,91,256]{4,1,3,2,0:T(2,128)S(1)}, u32[]{:S(2)}, u32[]{:S(2)}) %collective-permute-start.19) | collective-permute-done | bytes 1118240 | tf_op jit(solution)/shard_map/ppermute | solution.py:20
  702.9 2.9 fusion.407
  705.8 14.7 %all-reduce = (f32[2,3,180]{2,1,0:T(4,128)S(1)}, f32[2,3,180]{2,1,0:T(4,128)S(1)}) all-reduce(f32[2,3,180]{2,1,0:T(4,128)S(1)} %get-tuple-element.11, f32[2,3,180]{2,1,0:T(4,128)S(1)} %get-tuple-element.10), channel_id=1, replica_groups=mesh['space'=32,'feat'=4] {'feat'}, use_global_device_ids=true, to_apply=%region_15.16 | all-reduce | flops 2160 | bytes 17280 | tf_op jit(solution)/shard_map/psum | solution.py:168
  720.6 3.5 fusion.76
  (287 shorter events, 135.8 us)
Async XLA Ops:
  7.2 343.3 %copy-start = (bf16[1024,1024]{1,0:T(8,128)(2,1)S(1)}, bf16[1024,1024]{1,0:T(8,128)(2,1)}, u32[]{:S(2)}) copy-start(bf16[1024,1024]{1,0:T(8,128)(2,1)} %param.14) | copy-start | bytes 6291460
  7.2 21.5 %copy-start.2 = (bf16[2,3,180,256]{3,0,2,1:T(2,128)(2,1)S(1)}, bf16[2,3,180,256]{3,0,2,1:T(2,128)(2,1)}, u32[]{:S(2)}) copy-start(bf16[2,3,180,256]{3,0,2,1:T(2,128)(2,1)} %param.8) | copy-start | bytes 1658884
  7.2 340.1 %all-gather.3.cloned.1.call-start = ((), (), s32[]{:S(2)}) async-start(), calls=%async_computation.2 | async-start | bytes 2826240 | tf_op jit(solution)/shard_map/all_gather | solution.py:221
  32.8 24.4 %collective-permute-start = (f32[2,2,3,91,256]{4,1,3,2,0:T(2,128)}, f32[2,2,3,91,256]{4,1,3,2,0:T(2,128)S(1)}, u32[]{:S(2)}, u32[]{:S(2)}) collective-permute-start(f32[2,2,3,91,256]{4,1,3,2,0:T(2,128)} %copy.93), channel_id=1, source_target_pairs={{0,64},{64,0},{4,68},{68,4},{8,72},{72,8},{12,76},{76,12},{16,80},... | collective-permute-start | bytes 3354632 | tf_op jit(solution)/shard_map/ppermute | solution.py:20
  61.0 22.0 %collective-permute-start.1 = (f32[2,2,3,91,256]{4,1,3,2,0:T(2,128)}, f32[2,2,3,91,256]{4,1,3,2,0:T(2,128)}, u32[]{:S(2)}, u32[]{:S(2)}) collective-permute-start(f32[2,2,3,91,256]{4,1,3,2,0:T(2,128)} %copy.96), channel_id=1, source_target_pairs={{0,32},{32,0},{4,36},{36,4},{8,40},{40,8},{12,44},{44,12},{16,48},... | collective-permute-start | bytes 3354632 | tf_op jit(solution)/shard_map/ppermute | solution.py:20
  88.0 24.8 %copy-start.14 = (f32[2,3,91,256]{3,2,1,0:T(8,128)S(1)}, f32[2,3,91,256]{3,2,1,0:T(8,128)}, u32[]{:S(2)}) copy-start(f32[2,3,91,256]{3,2,1,0:T(8,128)} %copy-done.13) | copy-start | bytes 1677316
  88.0 24.8 %copy-start.16 = (f32[2,3,91,256]{3,2,1,0:T(8,128)S(1)}, f32[2,3,91,256]{3,2,1,0:T(8,128)}, u32[]{:S(2)}) copy-start(f32[2,3,91,256]{3,2,1,0:T(8,128)} %copy-done.15) | copy-start | bytes 1677316
  88.0 23.2 %collective-permute-start.2 = (f32[2,2,3,91,256]{4,1,3,2,0:T(2,128)}, f32[2,2,3,91,256]{4,1,3,2,0:T(2,128)}, u32[]{:S(2)}, u32[]{:S(2)}) collective-permute-start(f32[2,2,3,91,256]{4,1,3,2,0:T(2,128)} %copy.99), channel_id=1, source_target_pairs={{0,16},{16,0},{4,20},{20,4},{8,24},{24,8},{12,28},{28,12},{32,48},... | collective-permute-start | bytes 3354632 | tf_op jit(solution)/shard_map/ppermute | solution.py:20
  116.1 22.1 %copy-start.18 = (f32[2,3,91,256]{3,2,1,0:T(8,128)S(1)}, f32[2,3,91,256]{3,2,1,0:T(8,128)}, u32[]{:S(2)}) copy-start(f32[2,3,91,256]{3,2,1,0:T(8,128)} %copy-done.17) | copy-start | bytes 1677316
  116.1 20.5 %collective-permute-start.3 = (f32[2,2,3,91,256]{4,1,3,2,0:T(2,128)}, f32[2,2,3,91,256]{4,1,3,2,0:T(2,128)}, u32[]{:S(2)}, u32[]{:S(2)}) collective-permute-start(f32[2,2,3,91,256]{4,1,3,2,0:T(2,128)} %copy.102), channel_id=1, source_target_pairs={{0,8},{8,0},{4,12},{12,4},{16,24},{24,16},{20,28},{28,20},{32,40},... | collective-permute-start | bytes 3354632 | tf_op jit(solution)/shard_map/ppermute | solution.py:20
  142.4 3.3 collective-permute-start.4
  175.7 5.8 copy-start.29
  175.7 5.8 copy-start.52
  186.7 4.1 copy-start.25
  192.3 3.2 collective-permute-start.5
  197.3 26.8 %collective-permute-start.6 = (f32[2,2,3,91,256]{4,1,3,2,0:T(2,128)S(1)}, f32[2,2,3,91,256]{4,1,3,2,0:T(2,128)S(1)}, u32[]{:S(2)}, u32[]{:S(2)}) collective-permute-start(f32[2,2,3,91,256]{4,1,3,2,0:T(2,128)S(1)} %copy.135), channel_id=1, source_target_pairs={{0,8},{8,0},{4,12},{12,4},{16,24},{24,16},{20,28},{28,20},{32,40},... | collective-permute-start | bytes 3354632 | tf_op jit(solution)/shard_map/ppermute | solution.py:20
  225.9 27.4 %collective-permute-start.7 = (f32[2,2,3,91,256]{4,1,3,2,0:T(2,128)S(1)}, f32[2,2,3,91,256]{4,1,3,2,0:T(2,128)S(1)}, u32[]{:S(2)}, u32[]{:S(2)}) collective-permute-start(f32[2,2,3,91,256]{4,1,3,2,0:T(2,128)S(1)} %copy.138), channel_id=1, source_target_pairs={{0,16},{16,0},{4,20},{20,4},{8,24},{24,8},{12,28},{28,12},{32,48},... | collective-permute-start | bytes 3354632 | tf_op jit(solution)/shard_map/ppermute | solution.py:20
  255.1 25.0 %collective-permute-start.8 = (f32[2,2,3,91,256]{4,1,3,2,0:T(2,128)S(1)}, f32[2,2,3,91,256]{4,1,3,2,0:T(2,128)S(1)}, u32[]{:S(2)}, u32[]{:S(2)}) collective-permute-start(f32[2,2,3,91,256]{4,1,3,2,0:T(2,128)S(1)} %copy.141), channel_id=1, source_target_pairs={{0,32},{32,0},{4,36},{36,4},{8,40},{40,8},{12,44},{44,12},{16,48},... | collective-permute-start | bytes 3354632 | tf_op jit(solution)/shard_map/ppermute | solution.py:20
  281.9 25.6 %collective-permute-start.9 = (f32[2,2,3,91,256]{4,1,3,2,0:T(2,128)S(1)}, f32[2,2,3,91,256]{4,1,3,2,0:T(2,128)S(1)}, u32[]{:S(2)}, u32[]{:S(2)}) collective-permute-start(f32[2,2,3,91,256]{4,1,3,2,0:T(2,128)S(1)} %copy.144), channel_id=1, source_target_pairs={{0,64},{64,0},{4,68},{68,4},{8,72},{72,8},{12,76},{76,12},{16,80},... | collective-permute-start | bytes 3354632 | tf_op jit(solution)/shard_map/ppermute | solution.py:20
  312.0 73.8 %all-gather.5.cloned.1.call-start = ((), (), s32[]{:S(2)}) async-start(), calls=%async_computation.4 | async-start | bytes 2826240 | tf_op jit(solution)/shard_map/all_gather | solution.py:222
  314.3 113.5 %reduce-scatter.5.cloned.1.call-start = ((), (), s32[]{:S(2)}) async-start(), calls=%async_computation.5 | async-start | bytes 2826240 | tf_op jit(solution)/shard_map/reduce_scatter | solution.py:172
  395.6 32.2 %copy-start.5 = (bf16[2,3,180,256]{3,2,1,0:T(8,128)(2,1)S(1)}, bf16[2,3,180,256]{3,2,1,0:T(8,128)(2,1)}, u32[]{:S(2)}) copy-start(bf16[2,3,180,256]{3,2,1,0:T(8,128)(2,1)} %fusion.41) | copy-start | bytes 1658884
  395.6 32.2 %copy-start.42 = (f32[2,3,180]{2,1,0:T(4,128)S(1)}, f32[2,3,180]{2,1,0:T(4,128)}, u32[]{:S(2)}) copy-start(f32[2,3,180]{2,1,0:T(4,128)} %copy-done.41) | copy-start | bytes 12964
  395.6 32.2 %copy-start.45 = (f32[2,3,180]{2,1,0:T(4,128)S(1)}, f32[2,3,180]{2,1,0:T(4,128)}, u32[]{:S(2)}) copy-start(f32[2,3,180]{2,1,0:T(4,128)} %copy-done.44) | copy-start | bytes 12964
  395.6 49.2 %copy-start.36 = (bf16[2,3,180,256]{3,0,2,1:T(2,128)(2,1)S(1)}, bf16[2,3,180,256]{3,0,2,1:T(2,128)(2,1)}, u32[]{:S(2)}) copy-start(bf16[2,3,180,256]{3,0,2,1:T(2,128)(2,1)} %param.9) | copy-start | bytes 1658884
  395.6 324.9 %reduce-scatter.3.cloned.1.call-start = ((), (), s32[]{:S(2)}) async-start(), calls=%async_computation.3 | async-start | bytes 2826240 | tf_op jit(solution)/shard_map/reduce_scatter | solution.py:172
  427.8 17.0 %copy-start.33 = (bf16[2,3,180,256]{3,2,1,0:T(8,128)(2,1)S(1)}, bf16[2,3,180,256]{3,2,1,0:T(8,128)(2,1)}, u32[]{:S(2)}) copy-start(bf16[2,3,180,256]{3,2,1,0:T(8,128)(2,1)} %reduce-scatter.5.cloned.1.call-done) | copy-start | bytes 1658884
  444.8 256.2 %copy-start.47 = (f32[2,3,180]{2,1,0:T(4,128)}, f32[2,3,180]{2,1,0:T(4,128)S(1)}, u32[]{:S(2)}) copy-start(f32[2,3,180]{2,1,0:T(4,128)S(1)} %get-tuple-element.127) | copy-start | bytes 12964
  444.8 256.2 %copy-start.49 = (f32[2,3,180]{2,1,0:T(4,128)}, f32[2,3,180]{2,1,0:T(4,128)S(1)}, u32[]{:S(2)}) copy-start(f32[2,3,180]{2,1,0:T(4,128)S(1)} %get-tuple-element.128) | copy-start | bytes 12964
  449.1 24.5 %collective-permute-start.10 = (f32[2,2,3,91,256]{4,1,3,2,0:T(2,128)S(1)}, f32[2,2,3,91,256]{4,1,3,2,0:T(2,128)S(1)}, u32[]{:S(2)}, u32[]{:S(2)}) collective-permute-start(f32[2,2,3,91,256]{4,1,3,2,0:T(2,128)S(1)} %copy.149), channel_id=1, source_target_pairs={{0,64},{64,0},{4,68},{68,4},{8,72},{72,8},{12,76},{76,12},{16,80},... | collective-permute-start | bytes 3354632 | tf_op jit(solution)/shard_map/ppermute | solution.py:20
  475.2 22.4 %collective-permute-start.11 = (f32[2,2,3,91,256]{4,1,3,2,0:T(2,128)S(1)}, f32[2,2,3,91,256]{4,1,3,2,0:T(2,128)S(1)}, u32[]{:S(2)}, u32[]{:S(2)}) collective-permute-start(f32[2,2,3,91,256]{4,1,3,2,0:T(2,128)S(1)} %copy.152), channel_id=1, source_target_pairs={{0,32},{32,0},{4,36},{36,4},{8,40},{40,8},{12,44},{44,12},{16,48},... | collective-permute-start | bytes 3354632 | tf_op jit(solution)/shard_map/ppermute | solution.py:20
  499.2 24.0 %collective-permute-start.12 = (f32[2,2,3,91,256]{4,1,3,2,0:T(2,128)S(1)}, f32[2,2,3,91,256]{4,1,3,2,0:T(2,128)S(1)}, u32[]{:S(2)}, u32[]{:S(2)}) collective-permute-start(f32[2,2,3,91,256]{4,1,3,2,0:T(2,128)S(1)} %copy.155), channel_id=1, source_target_pairs={{0,16},{16,0},{4,20},{20,4},{8,24},{24,8},{12,28},{28,12},{32,48},... | collective-permute-start | bytes 3354632 | tf_op jit(solution)/shard_map/ppermute | solution.py:20
  524.8 21.6 %collective-permute-start.13 = (f32[2,2,3,91,256]{4,1,3,2,0:T(2,128)S(1)}, f32[2,2,3,91,256]{4,1,3,2,0:T(2,128)S(1)}, u32[]{:S(2)}, u32[]{:S(2)}) collective-permute-start(f32[2,2,3,91,256]{4,1,3,2,0:T(2,128)S(1)} %copy.158), channel_id=1, source_target_pairs={{0,8},{8,0},{4,12},{12,4},{16,24},{24,16},{20,28},{28,20},{32,40},... | collective-permute-start | bytes 3354632 | tf_op jit(solution)/shard_map/ppermute | solution.py:20
  548.0 3.2 collective-permute-start.14
  584.3 2.8 collective-permute-start.15
  588.9 26.8 %collective-permute-start.16 = (f32[2,2,3,91,256]{4,1,3,2,0:T(2,128)S(1)}, f32[2,2,3,91,256]{4,1,3,2,0:T(2,128)S(1)}, u32[]{:S(2)}, u32[]{:S(2)}) collective-permute-start(f32[2,2,3,91,256]{4,1,3,2,0:T(2,128)S(1)} %copy.189), channel_id=1, source_target_pairs={{0,8},{8,0},{4,12},{12,4},{16,24},{24,16},{20,28},{28,20},{32,40},... | collective-permute-start | bytes 3354632 | tf_op jit(solution)/shard_map/ppermute | solution.py:20
  616.6 32.6 %slice-start = ((s8[4521984]{0:T(1024)(128)(4,1)}), s8[4194304]{0:T(1024)(128)(4,1)S(1)}, s32[]{:S(2)}) async-start(s8[4521984]{0:T(1024)(128)(4,1)} %bitcast.747), calls=%async_computation.6 | async-start | bytes 8388608
  617.4 27.4 %collective-permute-start.17 = (f32[2,2,3,91,256]{4,1,3,2,0:T(2,128)S(1)}, f32[2,2,3,91,256]{4,1,3,2,0:T(2,128)S(1)}, u32[]{:S(2)}, u32[]{:S(2)}) collective-permute-start(f32[2,2,3,91,256]{4,1,3,2,0:T(2,128)S(1)} %copy.192), channel_id=1, source_target_pairs={{0,16},{16,0},{4,20},{20,4},{8,24},{24,8},{12,28},{28,12},{32,48},... | collective-permute-start | bytes 3354632 | tf_op jit(solution)/shard_map/ppermute | solution.py:20
  647.7 25.2 %collective-permute-start.18 = (f32[2,2,3,91,256]{4,1,3,2,0:T(2,128)}, f32[2,2,3,91,256]{4,1,3,2,0:T(2,128)S(1)}, u32[]{:S(2)}, u32[]{:S(2)}) collective-permute-start(f32[2,2,3,91,256]{4,1,3,2,0:T(2,128)} %copy.195), channel_id=1, source_target_pairs={{0,32},{32,0},{4,36},{36,4},{8,40},{40,8},{12,44},{44,12},{16,48},... | collective-permute-start | bytes 3354632 | tf_op jit(solution)/shard_map/ppermute | solution.py:20
  674.6 26.4 %copy-start.34 = (bf16[2,3,180,256]{3,2,1,0:T(8,128)(2,1)S(1)}, bf16[2,3,180,256]{3,2,1,0:T(8,128)(2,1)}, u32[]{:S(2)}) copy-start(bf16[2,3,180,256]{3,2,1,0:T(8,128)(2,1)} %reduce-scatter.5.cloned.1.call-done) | copy-start | bytes 1658884
  674.6 26.4 %copy-start.37 = (bf16[2,3,180,256]{3,0,2,1:T(2,128)(2,1)S(1)}, bf16[2,3,180,256]{3,0,2,1:T(2,128)(2,1)}, u32[]{:S(2)}) copy-start(bf16[2,3,180,256]{3,0,2,1:T(2,128)(2,1)} %param.9) | copy-start | bytes 1658884
  674.6 26.0 %collective-permute-start.19 = (f32[2,2,3,91,256]{4,1,3,2,0:T(2,128)S(1)}, f32[2,2,3,91,256]{4,1,3,2,0:T(2,128)S(1)}, u32[]{:S(2)}, u32[]{:S(2)}) collective-permute-start(f32[2,2,3,91,256]{4,1,3,2,0:T(2,128)S(1)} %copy.198), channel_id=1, source_target_pairs={{0,64},{64,0},{4,68},{68,4},{8,72},{72,8},{12,76},{76,12},{16,80},... | collective-permute-start | bytes 3354632 | tf_op jit(solution)/shard_map/ppermute | solution.py:20
  702.8 17.7 %copy-start.6 = (bf16[2,3,180,256]{3,2,1,0:T(8,128)(2,1)S(1)}, bf16[2,3,180,256]{3,2,1,0:T(8,128)(2,1)}, u32[]{:S(2)}) copy-start(bf16[2,3,180,256]{3,2,1,0:T(8,128)(2,1)} %fusion.41) | copy-start | bytes 1658884
  702.8 17.7 %copy-start.43 = (f32[2,3,180]{2,1,0:T(4,128)S(1)}, f32[2,3,180]{2,1,0:T(4,128)}, u32[]{:S(2)}) copy-start(f32[2,3,180]{2,1,0:T(4,128)} %copy-done.41) | copy-start | bytes 12964
  702.9 17.7 %copy-start.46 = (f32[2,3,180]{2,1,0:T(4,128)S(1)}, f32[2,3,180]{2,1,0:T(4,128)}, u32[]{:S(2)}) copy-start(f32[2,3,180]{2,1,0:T(4,128)} %copy-done.44) | copy-start | bytes 12964
  702.9 17.7 %copy-start.48 = (f32[2,3,180]{2,1,0:T(4,128)S(1)}, f32[2,3,180]{2,1,0:T(4,128)}, u32[]{:S(2)}) copy-start(f32[2,3,180]{2,1,0:T(4,128)} %copy-done.47) | copy-start | bytes 12964
  702.9 17.7 %copy-start.50 = (f32[2,3,180]{2,1,0:T(4,128)S(1)}, f32[2,3,180]{2,1,0:T(4,128)}, u32[]{:S(2)}) copy-start(f32[2,3,180]{2,1,0:T(4,128)} %copy-done.49) | copy-start | bytes 12964
  720.6 6.0 copy-start.1
  (35 other events, 72.4 us)
Sparse Core Ops, SparseCore 0:
  312.2 35.1 all-gather.2
  349.0 36.8 all-gather.4
  395.7 31.9 reduce-scatter.4
  653.0 27.3 reduce-scatter.2
where the time goes:
time: 744 us; the launch traced here: 734 us
  waiting for transfers between devices  459 us (62%)
  matrix products  90.5 us (12%)
  local copies, waits for them, and re-layouts  62.7 us (8%)
  blocking collectives  46.9 us (6%)
  starting transfers between devices  36.6 us (5%)
  other arithmetic  21.5 us (3%)
  between operations  16.3 us (2%)
    ppermute x20, waiting for transfers between devices, swapped(): return lax.ppermute(block, axis, route)  363 us
    psum x3, blocking collectives, token_sums(): return lax.psum((first_term, second_term), 'feat')  46.9 us
    dot_general x16, matrix products, lat_apply(): return jnp.einsum('gh,bhkc->bgkc', table, field, precision=HIGHEST)  36.6 us
    ppermute x20, starting transfers between devices, swapped(): return lax.ppermute(block, axis, route)  36.3 us
    all_gather x1, waiting for transfers between devices, per_device(): lax.all_gather(residual, 'feat', axis=3, tiled=True)  33 us
    reduce_scatter x2, waiting for transfers between devices, channel_share(): lax.psum_scatter(term.astype(jnp.bfloat16), 'feat', scatter_dimension=3,...  32.1 us
    all_gather x1, waiting for transfers between devices, per_device(): lax.all_gather(cotangent, 'feat', axis=3, tiled=True)  30.4 us
  transfers between devices with their start and end apart: 24, of which 23 were waited for; matrix products, arithmetic and copies ran while one was open for 3% of the time, Pallas kernels for 0%

commit v1 on v0

--- a/solution.py
+++ b/solution.py
@@ -8,16 +8,6 @@
 EPSILON = 1e-05
 SHRINK_LEVEL = 0.1
 HIGHEST = lax.Precision.HIGHEST
-
-
-def swapped(block, axis, bit):
-    count = lax.axis_size(axis)
-    route = []
-    for low in range(count):
-        high = low | 1 << bit
-        if high != low and high < count:
-            route += [(low, high), (high, low)]
-    return lax.ppermute(block, axis, route)
 
 
 def longitude_tables(width_lon):
@@ -36,9 +26,11 @@
     return (cos_fwd, sin_fwd, cos_fwd * doubled, sin_fwd * doubled)
 
 
-def padded_tables(width_lon):
+def padded_tables(width_lon, multiple):
     tables = longitude_tables(width_lon)
-    return tables
+    modes = tables[0].shape[1]
+    extra = -modes % multiple
+    return tuple(jnp.pad(table, ((0, 0), (0, extra))) for table in tables)
 
 
 def lat_apply(table, field):
@@ -91,77 +83,38 @@
     )
 
 
-def butterfly_level(real_part, imag_part, position, level_bit, inverse):
-    half_span = 1 << level_bit
-    is_upper = position >> level_bit & 1 == 1
-    offset = (position & half_span - 1).astype(jnp.float32)
-    phase_angle = math.pi / half_span * offset
-    cosine = jnp.cos(phase_angle)
-    sine_val = jnp.sin(phase_angle)
-    turned_real = real_part * cosine - imag_part * sine_val
-    turned_imag = imag_part * cosine + real_part * sine_val
-    if inverse:
-        outgoing = jnp.stack(
-            [
-                jnp.where(is_upper, turned_real, real_part),
-                jnp.where(is_upper, turned_imag, imag_part),
-            ]
-        )
-    else:
-        outgoing = jnp.stack([real_part, imag_part])
-    received = swapped(outgoing, "space", level_bit)
-    got_real = received[0]
-    got_imag = received[1]
-    if inverse:
-        upper_real = got_real - turned_real
-        upper_imag = got_imag - turned_imag
-    else:
-        diff_real = got_real - real_part
-        diff_imag = got_imag - imag_part
-        upper_real = diff_real * cosine + diff_imag * sine_val
-        upper_imag = diff_imag * cosine - diff_real * sine_val
-    return (
-        jnp.where(is_upper, upper_real, real_part + got_real),
-        jnp.where(is_upper, upper_imag, imag_part + got_imag),
-    )
-
-
-def butterfly_transform(real_part, imag_part, inverse):
-    nspace = lax.axis_size("space")
-    levels = nspace.bit_length() - 1
-    position = lax.axis_index("space")
-    row_count = real_part.shape[1]
-    length = row_count * nspace
-    frequency = jnp.zeros((), jnp.int32)
-    for level_bit in range(levels):
-        frequency = frequency + ((position >> level_bit & 1) << levels - 1 - level_bit)
-    out_index = jnp.arange(row_count, dtype=jnp.int32)[:, None]
-    in_index = jnp.arange(row_count, dtype=jnp.int32)[None, :]
-    wave_number = frequency + nspace * out_index
-    phase_angle = 2.0 * math.pi / length * (wave_number * in_index % length).astype(jnp.float32)
+def latitude_tables(length):
+    index_row = jnp.arange(length, dtype=jnp.int32)
+    phase_angle = (
+        2.0 * math.pi / length * (index_row[:, None] * index_row[None, :] % length).astype(jnp.float32)
+    )
     scaling = 1.0 / math.sqrt(length)
-    table_cos = jnp.cos(phase_angle) * scaling
-    table_sin = -jnp.sin(phase_angle) * scaling
-    if inverse:
-        real_part, imag_part = complex_latitude(
-            table_cos.T, table_sin.T, real_part, imag_part, True
-        )
-        for level_bit in range(levels):
-            real_part, imag_part = butterfly_level(real_part, imag_part, position, level_bit, True)
-        return (real_part, imag_part)
-    for level_bit in reversed(range(levels)):
-        real_part, imag_part = butterfly_level(real_part, imag_part, position, level_bit, False)
+    return (jnp.cos(phase_angle) * scaling, -jnp.sin(phase_angle) * scaling)
+
+
+def to_columns(real_part, imag_part):
+    stacked = jnp.stack([real_part, imag_part])
+    moved = lax.all_to_all(stacked, "space", 3, 2, tiled=True)
+    return (moved[0], moved[1])
+
+
+def to_rows(real_part, imag_part):
+    stacked = jnp.stack([real_part, imag_part])
+    moved = lax.all_to_all(stacked, "space", 2, 3, tiled=True)
+    return (moved[0], moved[1])
+
+
+def enter_spectrum(real_part, imag_part):
+    length = real_part.shape[1] * lax.axis_size("space")
+    table_cos, table_sin = latitude_tables(length)
+    real_part, imag_part = to_columns(real_part, imag_part)
     return complex_latitude(table_cos, table_sin, real_part, imag_part, False)
 
 
-def enter_spectrum(real_part, imag_part):
-    result = butterfly_transform(real_part, imag_part, False)
-    return result
-
-
 def leave_spectrum(real_part, imag_part):
-    result = butterfly_transform(real_part, imag_part, True)
-    return result
+    table_cos, table_sin = latitude_tables(real_part.shape[1])
+    real_part, imag_part = complex_latitude(table_cos, table_sin, real_part, imag_part, True)
+    return to_rows(real_part, imag_part)
 
 
 def token_sums(first_term, second_term):
@@ -187,7 +140,7 @@
 def per_device(inputs, cotangent, spec_w1, spec_b1, spec_w2, spec_b2, up_weight, down_weight):
     full_width = up_weight.shape[0]
     block_size = spec_w1.shape[2]
-    cos_fwd, sin_fwd, cos_inv, sin_inv = padded_tables(inputs.shape[2])
+    cos_fwd, sin_fwd, cos_inv, sin_inv = padded_tables(inputs.shape[2], lax.axis_size("space"))
     values = inputs.astype(jnp.float32)
     first_sum, second_sum = token_sums(jnp.sum(values, axis=-1), jnp.sum(values * values, axis=-1))
     mean_one = first_sum[..., None] / full_width

time: 744 us -> 344 us (0.46)
  waiting for transfers between devices: 459 us -> 139 us
  local copies, waits for them, and re-layouts: 62.7 us -> 21.4 us
  matrix products: 90.5 us -> 60.4 us
  blocking collectives: 46.9 us -> 69.7 us
  starting transfers between devices: 36.6 us -> 20.8 us
  other arithmetic: 21.5 us -> 11.9 us
    ppermute x20 -> x0, waiting for transfers between devices: 363 us -> none  [swapped(): return lax.ppermute(block, axis, route)]
    all_to_all x0 -> x3, waiting for transfers between devices: none -> 46.5 us  [the longest x2 29.4 us: to_columns(): moved = lax.all_to_all(stacked, 'space', 3, 2, tiled=True)]
    ppermute x20 -> x0, starting transfers between devices: 36.3 us -> none  [swapped(): return lax.ppermute(block, axis, route)]
    all_to_all x0 -> x1, blocking collectives: none -> 22.8 us  [to_rows(): moved = lax.all_to_all(stacked, 'space', 2, 3, tiled=True)]
    dot_general x16, matrix products: 36.6 us -> 14.4 us  [lat_apply(): return jnp.einsum('gh,bhkc->bgkc', table, field, precision=HIGHEST)]
    all_to_all x0 -> x3, starting transfers between devices: none -> 20.5 us  [the longest x2 15.8 us: to_columns(): moved = lax.all_to_all(stacked, 'space', 3, 2, tiled=True)]
    another operation x20 -> x4, local copies, waits for them, and re-layouts: 23.6 us -> 6.72 us  [the longest x2 3.87 us: to_columns(): stacked = jnp.stack([real_part, imag_part])]
    reshape x12 -> x0, local copies, waits for them, and re-layouts: 16 us -> none  [the longest x4 6.48 us: to_blocks(): field.reshape(field.shape[:-1] + (field.shape[-1] // block_size, block_si...]
  transfers between devices with their start and end apart: 24 -> 7, of which waited for: 23 -> 6; matrix products, arithmetic and copies ran while one was open for 3% -> 11% of each run, Pallas kernels for 0% -> 0%
where the time goes in v1:
time: 344 us; the launch traced here: 339 us
  waiting for transfers between devices  139 us (40%)
  blocking collectives  69.7 us (20%)
  matrix products  60.4 us (18%)
  local copies, waits for them, and re-layouts  21.4 us (6%)
  starting transfers between devices  20.8 us (6%)
  between operations  14.8 us (4%)
  other arithmetic  11.9 us (3%)
    psum x3, blocking collectives, token_sums(): return lax.psum((first_term, second_term), 'feat')  46.9 us
    reduce_scatter x2, waiting for transfers between devices, channel_share(): lax.psum_scatter(term.astype(jnp.bfloat16), 'feat', scatter_dimension=3,...  32.1 us
    all_gather x1, waiting for transfers between devices, per_device(): lax.all_gather(cotangent, 'feat', axis=3, tiled=True)  31 us
    all_gather x1, waiting for transfers between devices, per_device(): lax.all_gather(residual, 'feat', axis=3, tiled=True)  29.7 us
    all_to_all x2, waiting for transfers between devices, to_columns(): moved = lax.all_to_all(stacked, 'space', 3, 2, tiled=True)  29.4 us
    all_to_all x1, blocking collectives, to_rows(): moved = lax.all_to_all(stacked, 'space', 2, 3, tiled=True)  22.8 us
    all_to_all x1, waiting for transfers between devices, to_rows(): moved = lax.all_to_all(stacked, 'space', 2, 3, tiled=True)  17.2 us
    all_to_all x2, starting transfers between devices, to_columns(): moved = lax.all_to_all(stacked, 'space', 3, 2, tiled=True)  15.8 us
  transfers between devices with their start and end apart: 7, of which 6 were waited for; matrix products, arithmetic and copies ran while one was open for 11% of the time, Pallas kernels for 0%

profile of v1, /device:TPU:0, one launch (start us, length us, event | category | flops | bytes accessed | tf_op | source)
XLA Modules:
  0.0 338.6 jit_solution(17439749709295966867)
XLA Ops:
  8.0 1.6 convert_reduce_fusion.1
  9.6 17.3 %all-reduce.6 = (f32[2,3,180]{2,1,0:T(4,128)S(1)}, f32[2,3,180]{2,1,0:T(4,128)S(1)}) all-reduce(f32[2,3,180]{2,1,0:T(4,128)S(1)} %get-tuple-element.17, f32[2,3,180]{2,1,0:T(4,128)S(1)} %get-tuple-element.16), channel_id=1, replica_groups=mesh['space'=32,'feat'=4] {'feat'}, use_global_device_ids=true, to_apply=%region_3.4 | all-reduce | flops 2160 | bytes 17280 | tf_op jit(solution)/shard_map/psum | solution.py:121
  26.9 2.1 convolution_bitcast_fusion.5
  29.0 1.1 convolution_bitcast_fusion.4
  30.1 1.9 copy.108
  32.1 8.6 %all-to-all-start = ((f32[2,2,3,96,256]{4,1,2,0,3:T(2,128)}), f32[2,2,3,96,256]{4,1,2,0,3:T(2,128)}, u32[]{:S(2)}, u32[]{:S(2)}) async-start(f32[2,2,3,96,256]{4,1,2,0,3:T(2,128)} %copy.108), calls=%async_computation | async-start | bytes 2359296 | tf_op jit(solution)/shard_map/all_to_all | solution.py:97
  40.7 18.1 %all-to-all-done = f32[2,2,3,96,256]{4,1,2,0,3:T(2,128)} async-done(((f32[2,2,3,96,256]{4,1,2,0,3:T(2,128)}), f32[2,2,3,96,256]{4,1,2,0,3:T(2,128)}, u32[]{:S(2)}, u32[]{:S(2)}) %all-to-all-start) | async-done | bytes 1179680 | tf_op jit(solution)/shard_map/all_to_all | solution.py:97
  58.9 1.7 copy.109
  63.1 0.9 fusion.61
  69.9 0.9 fusion.88
  71.4 0.9 fusion.92
  72.3 0.9 fusion.52
  73.3 1.3 fusion.53
  74.6 1.9 copy.122
  76.6 4.7 %all-to-all-start.1 = ((f32[2,2,96,3,256]{4,1,3,0,2:T(2,128)}), f32[2,2,96,3,256]{4,1,3,0,2:T(2,128)}, u32[]{:S(2)}, u32[]{:S(2)}) async-start(f32[2,2,96,3,256]{4,1,3,0,2:T(2,128)} %copy.122), calls=%async_computation.1 | async-start | bytes 2359296 | tf_op jit(solution)/shard_map/all_to_all | solution.py:103
  81.3 1.1 fusion.201
  82.4 17.2 %all-to-all-done.1 = f32[2,2,96,3,256]{4,1,3,0,2:T(2,128)} async-done(((f32[2,2,96,3,256]{4,1,3,0,2:T(2,128)}), f32[2,2,96,3,256]{4,1,3,0,2:T(2,128)}, u32[]{:S(2)}, u32[]{:S(2)}) %all-to-all-start.1) | async-done | bytes 1179680 | tf_op jit(solution)/shard_map/all_to_all | solution.py:103
  99.6 1.7 copy.123
  102.6 1.0 fusion.109
  103.6 2.1 fusion.41
  105.8 1.9 copy.128
  107.8 29.7 %all-gather.3.cloned.1.call-done = bf16[2,3,180,1024]{3,2,1,0:T(8,128)(2,1)} async-done(((bf16[2,3,180,256]{3,2,1,0:T(8,128)(2,1)}), bf16[2,3,180,1024]{3,2,1,0:T(8,128)(2,1)}) %all-gather.3.cloned.1.call-update) | async-done | bytes 2211856 | tf_op jit(solution)/shard_map/all_gather | solution.py:174
  137.5 2.5 convert_reduce_fusion
  140.1 4.9 %fusion.12 = f32[2,3,180,1024]{3,2,1,0:T(8,128)} fusion(bf16[2,3,180,1024]{3,2,1,0:T(8,128)(2,1)S(1)} %copy-done.16, f32[2,3,180]{2,1,0:T(4,128)S(1)} %get-tuple-element.35, f32[2,3,180]{2,1,0:T(4,128)S(1)} %get-tuple-element.34, bf16[1024,1024]{1,0:T(8,128)(2,1)S(1)} %copy-done), kind=kOutput, calls=%fused_computation.17 | convolution fusion | flops 2269347840 | bytes 8741312 | tf_op jit(solution)/shard_map/brwd,dh->brwh/dot_general | solution.py:182
  145.0 31.0 %all-gather.5.cloned.1.call-done = bf16[2,3,180,1024]{3,2,1,0:T(8,128)(2,1)} async-done(((bf16[2,3,180,256]{3,2,1,0:T(8,128)(2,1)}), bf16[2,3,180,1024]{3,2,1,0:T(8,128)(2,1)}) %all-gather.5.cloned.1.call-update) | async-done | bytes 2211856 | tf_op jit(solution)/shard_map/all_gather | solution.py:175
  176.1 9.8 %fusion.28 = bf16[2,3,180,1024]{3,2,1,0:T(8,128)(2,1)} fusion(bf16[1024,1024]{1,0:T(8,128)(2,1)S(1)} %copy-done, f32[2,3,180,1024]{3,2,1,0:T(8,128)} %fusion.12, bf16[2,3,180,1024]{3,2,1,0:T(8,128)(2,1)} %all-gather.5.cloned.1.call-done, bf16[1024,1024]{1,0:T(8,128)(2,1)} %param.15), kind=kOutput, calls=%fused_computation.34 | convolution fusion | flops 4542013440 | bytes 13041664 | tf_op jit(solution)/shard_map/brwh,dh->brwd/dot_general | solution.py:194
  186.0 32.1 %reduce-scatter.5.cloned.1.call-done = bf16[2,3,180,256]{3,2,1,0:T(8,128)(2,1)} async-done(((bf16[2,3,180,1024]{3,2,1,0:T(8,128)(2,1)}), bf16[2,3,180,256]{3,2,1,0:T(8,128)(2,1)}) %reduce-scatter.5.cloned.1.call-update) | async-done | bytes 552976 | tf_op jit(solution)/shard_map/reduce_scatter | solution.py:125
  218.1 2.0 convert_reduce_fusion.2
  220.1 15.0 %all-reduce.5 = (f32[2,3,180]{2,1,0:T(4,128)S(1)}, f32[2,3,180]{2,1,0:T(4,128)S(1)}) all-reduce(f32[2,3,180]{2,1,0:T(4,128)S(1)} %get-tuple-element.15, f32[2,3,180]{2,1,0:T(4,128)S(1)} %get-tuple-element.14), channel_id=1, replica_groups=mesh['space'=32,'feat'=4] {'feat'}, use_global_device_ids=true, to_apply=%region_11.12 | all-reduce | flops 2160 | bytes 17280 | tf_op jit(solution)/shard_map/psum | solution.py:121
  235.1 1.6 convolution_bitcast_fusion.2
  236.8 1.6 convolution_bitcast_fusion.3
  238.5 1.9 copy.130
  240.5 7.2 %all-to-all-start.2 = ((f32[2,2,3,96,256]{4,1,2,0,3:T(2,128)}), f32[2,2,3,96,256]{4,1,2,0,3:T(2,128)S(1)}, u32[]{:S(2)}, u32[]{:S(2)}) async-start(f32[2,2,3,96,256]{4,1,2,0,3:T(2,128)} %copy.130), calls=%async_computation.4 | async-start | bytes 2359296 | tf_op jit(solution)/shard_map/all_to_all | solution.py:97
  247.9 6.9 %fusion.25 = bf16[2,3,180,1024]{3,2,1,0:T(8,128)(2,1)} fusion(bf16[1024,1024]{1,0:T(8,128)(2,1)} %param.15, f32[2,3,180,1024]{3,2,1,0:T(8,128)} %fusion.12), kind=kOutput, calls=%fused_computation.33 | convolution fusion | flops 2271559680 | bytes 8732672 | tf_op jit(solution)/shard_map/brwh,hd->brwd/dot_general | solution.py:186
  254.8 11.2 %all-to-all-done.2 = f32[2,2,3,96,256]{4,1,2,0,3:T(2,128)S(1)} async-done(((f32[2,2,3,96,256]{4,1,2,0,3:T(2,128)}), f32[2,2,3,96,256]{4,1,2,0,3:T(2,128)S(1)}, u32[]{:S(2)}, u32[]{:S(2)}) %all-to-all-start.2) | async-done | bytes 1179680 | tf_op jit(solution)/shard_map/all_to_all | solution.py:97
  267.1 0.9 fusion.131
  269.1 0.9 fusion.51
  276.9 0.9 fusion.44
  278.7 0.9 fusion.42
  280.4 0.9 fusion.43
  281.4 0.9 copy.142
  282.3 22.8 %all_to_all.60 = f32[2,2,96,3,256]{4,1,3,0,2:T(2,128)S(1)} all-to-all(f32[2,2,96,3,256]{4,1,3,0,2:T(2,128)S(1)} %copy.142), channel_id=1, replica_groups=mesh['space'=32,'feat'=4] {'space'}, dimensions={2} | all-to-all | bytes 2359296 | tf_op jit(solution)/shard_map/all_to_all | solution.py:103
  307.2 1.4 fusion.38
  308.6 2.4 fusion.355
  311.1 14.7 %all-reduce.4 = (f32[2,3,180]{2,1,0:T(4,128)S(1)}, f32[2,3,180]{2,1,0:T(4,128)S(1)}) all-reduce(f32[2,3,180]{2,1,0:T(4,128)S(1)} %get-tuple-element.13, f32[2,3,180]{2,1,0:T(4,128)S(1)} %get-tuple-element.12), channel_id=1, replica_groups=mesh['space'=32,'feat'=4] {'feat'}, use_global_device_ids=true, to_apply=%region_15.16 | all-reduce | flops 2160 | bytes 17280 | tf_op jit(solution)/shard_map/psum | solution.py:121
  325.8 3.5 %fusion.78 = (bf16[2,3,180,256]{3,2,1,0:T(8,128)(2,1)S(1)}, bf16[2,3,180,256]{3,2,1,0:T(8,128)(2,1)S(1)}) fusion(f32[2,3,180,256]{3,2,1,0:T(8,128)} %get-tuple-element.44, f32[2,3,180]{2,1,0:T(4,128)S(1)} %broadcast_multiply_fusion, f32[2,3,180]{2,1,0:T(4,128)S(1)} %broadcast_multiply_fusion.1, f32[2,3,180]{2,1,0:T(4,128)S(1)} %get-tuple-element.37, ...), kind=kLoop, calls=%fused_computation.106 | loop fusion | flops 6082560 | bytes 5011200 | tf_op jit(solution)/shard_map/convert_element_type | solution.py:230
  329.4 1.2 copy.149
  330.6 1.2 copy.148
  (117 shorter events, 24.6 us)
Async XLA Ops:
  7.2 132.9 %copy-start = (bf16[1024,1024]{1,0:T(8,128)(2,1)S(1)}, bf16[1024,1024]{1,0:T(8,128)(2,1)}, u32[]{:S(2)}) copy-start(bf16[1024,1024]{1,0:T(8,128)(2,1)} %param.14) | copy-start | bytes 6291460
  7.2 21.8 %copy-start.2 = (bf16[2,3,180,256]{3,0,2,1:T(2,128)(2,1)S(1)}, bf16[2,3,180,256]{3,0,2,1:T(2,128)(2,1)}, u32[]{:S(2)}) copy-start(bf16[2,3,180,256]{3,0,2,1:T(2,128)(2,1)} %param.8) | copy-start | bytes 1658884
  7.6 22.5 %copy-start.19 = (f32[180,91]{1,0:T(8,128)}, f32[180,91]{1,0:T(8,128)S(1)}, u32[]{:S(2)}) copy-start(f32[180,91]{1,0:T(8,128)S(1)} %fusion.202) | copy-start | bytes 196564
  8.0 22.1 %copy-start.25 = (f32[180,91]{1,0:T(8,128)}, f32[180,91]{1,0:T(8,128)S(1)}, u32[]{:S(2)}) copy-start(f32[180,91]{1,0:T(8,128)S(1)} %fusion.198) | copy-start | bytes 196564
  32.1 8.6 %copy-start.27 = (f32[2,256]{1,0:T(2,128)S(1)}, f32[2,256]{1,0:T(2,128)}, u32[]{:S(2)}) copy-start(f32[2,256]{1,0:T(2,128)} %param.11) | copy-start | bytes 6148
  32.1 8.6 %copy-start.28 = (f32[2,256]{1,0:T(2,128)S(1)}, f32[2,256]{1,0:T(2,128)}, u32[]{:S(2)}) copy-start(f32[2,256]{1,0:T(2,128)} %param.13) | copy-start | bytes 6148
  32.1 26.8 %all-to-all-start = ((f32[2,2,3,96,256]{4,1,2,0,3:T(2,128)}), f32[2,2,3,96,256]{4,1,2,0,3:T(2,128)}, u32[]{:S(2)}, u32[]{:S(2)}) async-start(f32[2,2,3,96,256]{4,1,2,0,3:T(2,128)} %copy.108), calls=%async_computation | async-start | bytes 2359296 | tf_op jit(solution)/shard_map/all_to_all | solution.py:97
  63.1 1.0 copy-start.12
  66.2 1.0 copy-start.11
  67.2 1.3 copy-start.7
  69.2 1.6 copy-start.5
  69.9 3.4 %copy-start.3 = (f32[2,96,3,2,128]{4,1,2,0,3:T(8,128)}, f32[2,96,3,2,128]{4,1,2,0,3:T(8,128)S(1)}, u32[]{:S(2)}) copy-start(f32[2,96,3,2,128]{4,1,2,0,3:T(8,128)S(1)} %fusion.55) | copy-start | bytes 1769476
  76.6 23.0 %all-to-all-start.1 = ((f32[2,2,96,3,256]{4,1,3,0,2:T(2,128)}), f32[2,2,96,3,256]{4,1,3,0,2:T(2,128)}, u32[]{:S(2)}, u32[]{:S(2)}) async-start(f32[2,2,96,3,256]{4,1,3,0,2:T(2,128)} %copy.122), calls=%async_computation.1 | async-start | bytes 2359296 | tf_op jit(solution)/shard_map/all_to_all | solution.py:103
  81.3 56.3 %all-gather.3.cloned.1.call-start = ((), (), s32[]{:S(2)}) async-start(), calls=%async_computation.6 | async-start | bytes 2826240 | tf_op jit(solution)/shard_map/all_gather | solution.py:174
  101.7 0.9 copy-start.21
  102.1 1.5 copy-start.23
  105.8 70.3 %all-gather.5.cloned.1.call-start = ((), (), s32[]{:S(2)}) async-start(), calls=%async_computation.8 | async-start | bytes 2826240 | tf_op jit(solution)/shard_map/all_gather | solution.py:175
  107.8 110.3 %reduce-scatter.5.cloned.1.call-start = ((), (), s32[]{:S(2)}) async-start(), calls=%async_computation.9 | async-start | bytes 2826240 | tf_op jit(solution)/shard_map/reduce_scatter | solution.py:125
  137.5 2.6 copy-start.16
  185.9 32.2 %copy-start.9 = (bf16[2,3,180,256]{3,2,1,0:T(8,128)(2,1)S(1)}, bf16[2,3,180,256]{3,2,1,0:T(8,128)(2,1)}, u32[]{:S(2)}) copy-start(bf16[2,3,180,256]{3,2,1,0:T(8,128)(2,1)} %fusion.41) | copy-start | bytes 1658884
  185.9 49.2 %copy-start.17 = (bf16[2,3,180,256]{3,0,2,1:T(2,128)(2,1)S(1)}, bf16[2,3,180,256]{3,0,2,1:T(2,128)(2,1)}, u32[]{:S(2)}) copy-start(bf16[2,3,180,256]{3,0,2,1:T(2,128)(2,1)} %param.9) | copy-start | bytes 1658884
  185.9 49.2 %copy-start.24 = (f32[180,91]{1,0:T(8,128)S(1)}, f32[180,91]{1,0:T(8,128)}, u32[]{:S(2)}) copy-start(f32[180,91]{1,0:T(8,128)} %get-tuple-element.42) | copy-start | bytes 196564
  218.1 17.0 %copy-start.14 = (bf16[2,3,180,256]{3,2,1,0:T(8,128)(2,1)S(1)}, bf16[2,3,180,256]{3,2,1,0:T(8,128)(2,1)}, u32[]{:S(2)}) copy-start(bf16[2,3,180,256]{3,2,1,0:T(8,128)(2,1)} %reduce-scatter.5.cloned.1.call-done) | copy-start | bytes 1658884
  235.1 1.7 copy-start.22
  240.5 25.6 %all-to-all-start.2 = ((f32[2,2,3,96,256]{4,1,2,0,3:T(2,128)}), f32[2,2,3,96,256]{4,1,2,0,3:T(2,128)S(1)}, u32[]{:S(2)}, u32[]{:S(2)}) async-start(f32[2,2,3,96,256]{4,1,2,0,3:T(2,128)} %copy.130), calls=%async_computation.4 | async-start | bytes 2359296 | tf_op jit(solution)/shard_map/all_to_all | solution.py:97
  247.7 78.1 %reduce-scatter.3.cloned.1.call-start = ((), (), s32[]{:S(2)}) async-start(), calls=%async_computation.7 | async-start | bytes 2826240 | tf_op jit(solution)/shard_map/reduce_scatter | solution.py:125
  269.9 1.1 copy-start.4
  271.7 1.1 copy-start.8
  272.8 1.0 copy-start.13
  273.8 1.1 copy-start.6
  305.9 1.1 copy-start.15
  305.9 1.2 copy-start.18
  306.0 1.2 copy-start.26
  307.2 1.4 copy-start.20
  308.6 17.2 %copy-start.10 = (bf16[2,3,180,256]{3,2,1,0:T(8,128)(2,1)S(1)}, bf16[2,3,180,256]{3,2,1,0:T(8,128)(2,1)}, u32[]{:S(2)}) copy-start(bf16[2,3,180,256]{3,2,1,0:T(8,128)(2,1)} %fusion.41) | copy-start | bytes 1658884
  325.8 6.0 %copy-start.1 = (bf16[1024,1024]{1,0:T(8,128)(2,1)S(1)}, bf16[1024,1024]{1,0:T(8,128)(2,1)}, u32[]{:S(2)}) copy-start(bf16[1024,1024]{1,0:T(8,128)(2,1)} %param.14) | copy-start | bytes 6291460
Sparse Core Ops, SparseCore 0:
  105.9 31.6 all-gather.2
  139.2 36.8 all-gather.4
  186.1 31.9 reduce-scatter.4
  255.0 30.2 reduce-scatter.2
